TPU v7x, 32 devices: a whole 2x2x4 slice. The times are simulated.
32 devices in a mesh: rep: 2 (over x), tm: 8 (over z, y), mp: 2 (over core).
Axes of the slice: x: 2, y: 2, z: 4, core: 2. Of those that a mesh axis runs over, the one named last changes fastest.
Arguments:
- inputs: bfloat16 [8, 1024, 1024], P('rep', 'tm'), parts along dimension 0, may hold values from -6 to 6
- resets: int32 [8, 1024], P('rep', 'tm'), parts along dimension 0, may hold values 0 or 1
- actions: int32 [8, 8, 128, 4], P('rep', None, 'tm'), parts along dimension 0, may hold values from 0 to 17
- in_proj: bfloat16 [1024, 1024], P(None, 'mp'), may hold values from -0.1875 to 0.1875
- decay_rates: float32 [1024], replicated, may hold values from 0.00024414062 to 0.03
- readout_w: bfloat16 [1024, 1024], P('mp'), may hold values from -0.1875 to 0.1875
- norm_gain: float32 [1024], replicated, may hold values from 0.1 to 1.9
- w_hidden: bfloat16 [1024, 1024], P(None, 'mp'), may hold values from -0.1875 to 0.1875
- action_embed: bfloat16 [18, 1024], P(None, 'mp'), may hold values from -6 to 6
- w_out: bfloat16 [1024, 1024], P('mp'), may hold values from -0.1875 to 0.1875
Outputs:
- predicted: bfloat16 [8, 8, 128, 4, 1024], P('rep', None, 'tm', None, 'mp'), parts along dimension 0
There are 2 independent parts, one for each index of `rep`. A program takes and returns all parts, laid end to end along the dimension named above; an argument that names none is the same for every part. Nothing has to cross between parts.
All inputs are finite; a program needn't handle non-finite values. No bound on the sum of `resets` on one device may be relied on, other than what follows from the above.
Results may differ from a plain program's by a relative error of at most 0.015.
Values may be sent and summed in bfloat16 or wider, within the bound.
No kernel may reach another device: no remote copies, remote signals or barrier semaphores. Data moves between devices by JAX's collectives and lax.ppermute only.
A program may use at most 64 MiB of HBM per device.

v0:
```python
import jax
import jax.numpy as jnp
from jax import lax
from jax.sharding import PartitionSpec as P


def carried_in(value, axis, join, neutral):
    count, mine = (lax.axis_size(axis), lax.axis_index(axis))
    pieces = jax.tree.map(lambda part: lax.all_gather(part, axis), value)
    total = jax.tree.map(
        lambda part, zero: jnp.full_like(part, 0) + jnp.asarray(zero, part.dtype), value, neutral
    )

    def hop(position, total):
        longer = join(total, jax.tree.map(lambda part: part[position], pieces))
        return jax.tree.map(lambda new, old: jnp.where(position < mine, new, old), longer, total)

    return lax.fori_loop(0, count - 1, hop, total)


def shortened(value):

    def short(part):
        return part.astype(jnp.bfloat16) if part.dtype == jnp.float32 else part

    return jax.tree.map(short, value)


def combine(earlier, later):
    return (earlier[0] * later[0], later[0] * earlier[1] + later[1])


def hidden_units(features, norm_gain, w_hidden, action_embed, picked):
    mean_sq = jnp.mean(features * features, axis=-1, keepdims=True)
    normed = (features * lax.rsqrt(mean_sq + 1e-06) * norm_gain).astype(jnp.bfloat16)
    table_ids = jnp.arange(action_embed.shape[0], dtype=jnp.int32)
    one_hot = (picked[:, None] == table_ids[None, :]).astype(jnp.bfloat16)
    pre_act = jnp.dot(normed, w_hidden, preferred_element_type=jnp.float32) + jnp.dot(
        one_hot, action_embed, preferred_element_type=jnp.float32
    )
    return jax.nn.silu(pre_act).astype(jnp.bfloat16)


def per_device(
    inputs,
    resets,
    actions,
    in_proj,
    decay_rates,
    readout_w,
    norm_gain,
    w_hidden,
    action_embed,
    w_out,
):
    mp_index = lax.axis_index("mp")
    width_part = in_proj.shape[1]
    local_rates = lax.dynamic_slice_in_dim(decay_rates, mp_index * width_part, width_part)
    decays = jnp.exp(-local_rates)
    scaling = jnp.sqrt(1.0 - decays * decays)
    batch, steps, width = inputs.shape
    driven = (
        jnp.dot(
            inputs.reshape(batch * steps, width), in_proj, preferred_element_type=jnp.float32
        ).reshape(batch, steps, width_part)
        * scaling
    )
    keep_mask = (1 - resets).astype(jnp.float32)
    gates = keep_mask[:, :, None] * decays
    cumulative, local_states = lax.associative_scan(combine, (gates, driven), axis=1)
    identity = (
        jnp.ones((batch, width_part), jnp.float32),
        jnp.zeros((batch, width_part), jnp.float32),
    )
    entering = carried_in((cumulative[:, -1], local_states[:, -1]), "tm", combine, identity)
    carry_state = entering[1]
    corrected = local_states + cumulative * carry_state[:, None, :]
    posterior = lax.all_to_all(
        shortened(corrected.reshape(batch, 1, steps, width_part)),
        "tm",
        split_axis=2,
        concat_axis=1,
        tiled=True,
    )
    seqs, blocks, sub_steps, horizon = actions.shape
    rows = seqs * blocks * sub_steps
    current = posterior.reshape(rows, width_part)
    action_rows = actions.reshape(rows, horizon)
    outputs = []
    for step in range(horizon):
        features = lax.psum(
            jnp.dot(
                current.astype(jnp.bfloat16), readout_w, preferred_element_type=jnp.float32
            ).astype(jnp.bfloat16),
            "mp",
        ).astype(jnp.float32)
        hidden = hidden_units(features, norm_gain, w_hidden, action_embed, action_rows[:, step])
        guessed = lax.psum_scatter(
            jnp.dot(hidden, w_out, preferred_element_type=jnp.float32).astype(jnp.bfloat16),
            "mp",
            scatter_dimension=1,
            tiled=True,
        )
        outputs.append(guessed)
        if step < horizon - 1:
            full_guess = lax.all_gather(guessed, "mp", axis=1, tiled=True)
            current = decays * current + scaling * jnp.dot(
                full_guess, in_proj, preferred_element_type=jnp.float32
            )
    result = jnp.stack(outputs, axis=1)
    return result.reshape(seqs, blocks, sub_steps, horizon, result.shape[2])


def solution(mesh):
    in_specs = (
        P("rep", "tm", None),
        P("rep", "tm"),
        P("rep", None, "tm", None),
        P(None, "mp"),
        P(),
        P("mp", None),
        P(),
        P(None, "mp"),
        P(None, "mp"),
        P("mp", None),
    )
    out_specs = P("rep", None, "tm", None, "mp")
    return jax.shard_map(
        per_device, mesh=mesh, in_specs=in_specs, out_specs=out_specs, check_vma=False
    )
```

profile of v0, /device:TPU:0, one launch (start us, length us, event | category | flops | bytes accessed | tf_op | source)
XLA Modules:
  0.0 339.0 jit_solution(1014321069220786846)
XLA Ops:
  8.8 1.5 slice.219
  10.3 2.2 convolution_multiply_fusion.3
  12.6 1.5 slice.268
  14.1 1.5 slice.222
  15.6 1.5 slice.221
  17.1 1.4 multiply_add_fusion
  25.9 1.2 fusion.36
  29.0 2.0 pad.98
  31.0 4.3 %pad.99 = f32[4,128,512]{2,1,0:T(8,128)} pad(f32[4,64,512]{2,1,0:T(8,128)} %add.272, f32[]{:T(128)} %constant.52.clone.1), padding=0_0_0x1_0_1x0_0_0 | pad | bytes 1572868 | tf_op jit(solution)/shard_map/pad | solution.py:70
  36.2 32.4 %all-gather.1 = f32[32,1,512]{2,1,0:T(1,128)S(1)} all-gather(f32[4,1,512]{2,1,0:T(1,128)S(1)} %slice_add_fusion), channel_id=3, replica_groups=mesh['rep'=2,'tm'=8,'mp'=2] {'tm'}, dimensions={0}, use_global_device_ids=true | all-gather | bytes 73728 | tf_op jit(solution)/shard_map/all_gather | solution.py:9
  68.7 4.3 %pad.113 = f32[4,128,512]{2,1,0:T(8,128)} pad(f32[4,64,512]{2,1,0:T(8,128)} %add.280, f32[]{:T(128)} %constant.52.clone.1), padding=0_0_0x1_0_1x0_0_0 | pad | bytes 1572868 | tf_op jit(solution)/shard_map/pad | solution.py:70
  73.8 30.7 %all-gather = f32[32,1,512]{2,1,0:T(1,128)S(1)} all-gather(f32[4,1,512]{2,1,0:T(1,128)S(1)} %slice_add_fusion.1), channel_id=2, replica_groups=mesh['rep'=2,'tm'=8,'mp'=2] {'tm'}, dimensions={0}, use_global_device_ids=true | all-gather | bytes 73728 | tf_op jit(solution)/shard_map/all_gather | solution.py:9
  105.0 2.0 fusion.35
  107.5 15.5 %all_to_all.4 = bf16[4,1,128,512]{3,0,1,2:T(4,128)(2,1)S(1)} all-to-all(bf16[4,1,128,512]{3,0,1,2:T(4,128)(2,1)S(1)} %copy.20), channel_id=1, replica_groups=mesh['rep'=2,'tm'=8,'mp'=2] {'tm'}, dimensions={2} | all-to-all | bytes 1048576 | tf_op jit(solution)/shard_map/all_to_all | solution.py:78
  123.9 1.7 convolution_convert_fusion.7
  125.7 18.4 %all-reduce.33.cloned.1.call-done = bf16[512,1024]{1,0:T(8,128)(2,1)} async-done(((bf16[512,1024]{1,0:T(8,128)(2,1)}), bf16[512,1024]{1,0:T(8,128)(2,1)}) %all-reduce.33.cloned.1.call-update) | async-done | bytes 1048592 | tf_op jit(solution)/shard_map/psum | solution.py:91
  144.1 1.5 fusion.1
  145.7 3.0 fusion.23
  148.6 3.7 %convolution_convert_fusion.6 = bf16[512,1024]{1,0:T(8,128)(2,1)} fusion(bf16[512,1024]{1,0:T(8,128)(2,1)} %param.21, f32[512,512]{1,0:T(8,128)} %fusion.23, bf16[18,512]{1,0:T(8,128)(2,1)S(1)} %copy-done.16, s32[512]{0:T(512)S(1)} %bitcast.91), kind=kOutput, calls=%fused_computation.30 | convolution fusion | flops 548414464 | bytes 3166208 | tf_op jit(solution)/shard_map/dot_general | solution.py:99
  152.4 9.7 %reduce-scatter.5.cloned.1.call-done = bf16[512,512]{1,0:T(8,128)(2,1)} async-done(((bf16[512,1024]{1,0:T(8,128)(2,1)}), bf16[512,512]{1,0:T(8,128)(2,1)}) %reduce-scatter.5.cloned.1.call-update) | async-done | bytes 524304 | tf_op jit(solution)/shard_map/reduce_scatter | solution.py:98
  162.1 11.7 %all-gather.6.cloned.1.call-done = bf16[512,1024]{1,0:T(8,128)(2,1)} async-done(((bf16[512,512]{1,0:T(8,128)(2,1)}), bf16[512,1024]{1,0:T(8,128)(2,1)}) %all-gather.6.cloned.1.call-update) | async-done | bytes 1048592 | tf_op jit(solution)/shard_map/all_gather | solution.py:106
  173.9 2.1 fusion.15
  175.9 1.7 convolution_convert_fusion.5
  177.9 20.5 %all-reduce.35.cloned.1.call-done = bf16[512,1024]{1,0:T(8,128)(2,1)} async-done(((bf16[512,1024]{1,0:T(8,128)(2,1)}), bf16[512,1024]{1,0:T(8,128)(2,1)}) %all-reduce.35.cloned.1.call-update) | async-done | bytes 1048592 | tf_op jit(solution)/shard_map/psum | solution.py:91
  198.4 1.5 fusion.4
  199.9 3.0 fusion.21
  202.9 3.6 %convolution_convert_fusion.4 = bf16[512,1024]{1,0:T(8,128)(2,1)} fusion(bf16[512,1024]{1,0:T(8,128)(2,1)} %param.21, f32[512,512]{1,0:T(8,128)} %fusion.21, bf16[18,512]{1,0:T(8,128)(2,1)S(1)} %copy-done.16, s32[512]{0:T(512)S(1)} %bitcast.90), kind=kOutput, calls=%fused_computation.28 | convolution fusion | flops 548414464 | bytes 3166208 | tf_op jit(solution)/shard_map/dot_general | solution.py:99
  206.5 9.7 %reduce-scatter.7.cloned.1.call-done = bf16[512,512]{1,0:T(8,128)(2,1)} async-done(((bf16[512,1024]{1,0:T(8,128)(2,1)}), bf16[512,512]{1,0:T(8,128)(2,1)}) %reduce-scatter.7.cloned.1.call-update) | async-done | bytes 524304 | tf_op jit(solution)/shard_map/reduce_scatter | solution.py:98
  216.3 11.6 %all-gather.8.cloned.1.call-done = bf16[512,1024]{1,0:T(8,128)(2,1)} async-done(((bf16[512,512]{1,0:T(8,128)(2,1)}), bf16[512,1024]{1,0:T(8,128)(2,1)}) %all-gather.8.cloned.1.call-update) | async-done | bytes 1048592 | tf_op jit(solution)/shard_map/all_gather | solution.py:106
  227.9 2.2 fusion.14
  230.1 1.7 convolution_convert_fusion.3
  231.9 20.7 %all-reduce.37.cloned.1.call-done = bf16[512,1024]{1,0:T(8,128)(2,1)} async-done(((bf16[512,1024]{1,0:T(8,128)(2,1)}), bf16[512,1024]{1,0:T(8,128)(2,1)}) %all-reduce.37.cloned.1.call-update) | async-done | bytes 1048592 | tf_op jit(solution)/shard_map/psum | solution.py:91
  252.6 1.5 fusion.7
  254.1 3.0 fusion.19
  257.1 3.7 %convolution_convert_fusion.2 = bf16[512,1024]{1,0:T(8,128)(2,1)} fusion(bf16[512,1024]{1,0:T(8,128)(2,1)} %param.21, f32[512,512]{1,0:T(8,128)} %fusion.19, bf16[18,512]{1,0:T(8,128)(2,1)S(1)} %copy-done.16, s32[512]{0:T(512)S(1)} %bitcast.89), kind=kOutput, calls=%fused_computation.26 | convolution fusion | flops 548414464 | bytes 3166208 | tf_op jit(solution)/shard_map/dot_general | solution.py:99
  260.8 9.7 %reduce-scatter.9.cloned.1.call-done = bf16[512,512]{1,0:T(8,128)(2,1)} async-done(((bf16[512,1024]{1,0:T(8,128)(2,1)}), bf16[512,512]{1,0:T(8,128)(2,1)}) %reduce-scatter.9.cloned.1.call-update) | async-done | bytes 524304 | tf_op jit(solution)/shard_map/reduce_scatter | solution.py:98
  270.6 11.7 %all-gather.10.cloned.1.call-done = bf16[512,1024]{1,0:T(8,128)(2,1)} async-done(((bf16[512,512]{1,0:T(8,128)(2,1)}), bf16[512,1024]{1,0:T(8,128)(2,1)}) %all-gather.10.cloned.1.call-update) | async-done | bytes 1048592 | tf_op jit(solution)/shard_map/all_gather | solution.py:106
  282.3 3.5 %convolution_convert_fusion.1 = bf16[512,1024]{1,0:T(8,128)(2,1)} fusion(bf16[512,1024]{1,0:T(8,128)(2,1)S(1)} %copy-done, bf16[512,1024]{1,0:T(8,128)(2,1)} %all-gather.10.cloned.1.call-done, bf16[1024,512]{1,0:T(8,128)(2,1)S(1)} %copy-done.8, f32[512,512]{1,0:T(8,128)S(1)} %fusion.14, f32[512]{0:T(512)S(1)} %get-tuple-element.128, ...), kind=kOutput, calls=%fused_computation.25 | convolution fusion | flops 1075314688 | bytes 5246976 | tf_op jit(solution)/shard_map/dot_general | solution.py:92
  285.8 20.7 %all-reduce.39.cloned.1.call-done = bf16[512,1024]{1,0:T(8,128)(2,1)} async-done(((bf16[512,1024]{1,0:T(8,128)(2,1)}), bf16[512,1024]{1,0:T(8,128)(2,1)}) %all-reduce.39.cloned.1.call-update) | async-done | bytes 1048592 | tf_op jit(solution)/shard_map/psum | solution.py:91
  306.5 1.5 fusion.10
  308.0 3.0 fusion.17
  311.0 3.7 %convolution_convert_fusion = bf16[512,1024]{1,0:T(8,128)(2,1)} fusion(bf16[512,1024]{1,0:T(8,128)(2,1)} %param.21, f32[512,512]{1,0:T(8,128)} %fusion.17, bf16[18,512]{1,0:T(8,128)(2,1)S(1)} %copy-done.16, s32[512]{0:T(512)S(1)} %bitcast.88), kind=kOutput, calls=%fused_computation.24 | convolution fusion | flops 548414464 | bytes 3166208 | tf_op jit(solution)/shard_map/dot_general | solution.py:99
  314.7 1.0 copy.23
  315.7 2.1 copy.24
  317.8 2.0 copy.25
  319.9 4.5 %reduce-scatter.11.cloned.1.call-done = bf16[512,512]{1,0:T(8,128)(2,1)} async-done(((bf16[512,1024]{1,0:T(8,128)(2,1)}), bf16[512,512]{1,0:T(8,128)(2,1)}) %reduce-scatter.11.cloned.1.call-update) | async-done | bytes 524304 | tf_op jit(solution)/shard_map/reduce_scatter | solution.py:98
  324.4 2.2 copy.26
  326.6 5.9 %pad_maximum_fusion = bf16[4,8,16,4,512]{4,3,2,1,0:T(4,128)(2,1)} fusion(bf16[4,8,16,1,512]{4,3,2,1,0:T(2,128)(2,1)S(1)} %copy.26, bf16[4,8,16,1,512]{4,3,2,1,0:T(2,128)(2,1)S(1)} %copy-done.1, bf16[4,8,16,1,512]{4,3,2,1,0:T(2,128)(2,1)S(1)} %copy.24, bf16[4,8,16,1,512]{4,3,2,1,0:T(2,128)(2,1)S(1)} %copy.23), kind=kLoop, calls=%fused_computation.23 | loop fusion | flops 8388608 | bytes 4194304 | tf_op jit(solution)/shard_map/stack | solution.py:110
  (179 shorter events, 15.7 us)
Async XLA Ops:
  6.5 117.3 %copy-start = (bf16[512,1024]{1,0:T(8,128)(2,1)S(1)}, bf16[512,1024]{1,0:T(8,128)(2,1)}, u32[]{:S(2)}) copy-start(bf16[512,1024]{1,0:T(8,128)(2,1)} %param.17) | copy-start | bytes 3145732
  6.5 137.6 %all-reduce.33.cloned.1.call-start = ((), (), s32[]{:S(2)}) async-start(), calls=%async_computation.5 | async-start | bytes 2097152 | tf_op jit(solution)/shard_map/psum | solution.py:91
  22.4 1.0 copy-start.9
  24.1 1.8 copy-start.4
  24.1 1.8 copy-start.5
  27.1 1.0 copy-start.6
  123.1 0.8 copy-start.10
  123.1 2.5 copy-start.11
  123.8 21.8 %copy-start.12 = (bf16[1024,512]{1,0:T(8,128)(2,1)S(1)}, bf16[1024,512]{1,0:T(8,128)(2,1)}, u32[]{:S(2)}) copy-start(bf16[1024,512]{1,0:T(8,128)(2,1)} %param.19) | copy-start | bytes 3145732
  123.9 21.8 %copy-start.17 = (f32[1024]{0:T(1024)S(1)}, f32[1024]{0:T(1024)}, u32[]{:S(2)}) copy-start(f32[1024]{0:T(1024)} %param.18) | copy-start | bytes 12292
  125.6 36.5 %reduce-scatter.5.cloned.1.call-start = ((), (), s32[]{:S(2)}) async-start(), calls=%async_computation.6 | async-start | bytes 1572864 | tf_op jit(solution)/shard_map/reduce_scatter | solution.py:98
  145.6 3.0 copy-start.16
  148.6 25.2 %copy-start.7 = (bf16[1024,512]{1,0:T(8,128)(2,1)S(1)}, bf16[1024,512]{1,0:T(8,128)(2,1)}, u32[]{:S(2)}) copy-start(bf16[1024,512]{1,0:T(8,128)(2,1)} %param.15) | copy-start | bytes 3145732
  152.3 21.5 %all-gather.6.cloned.1.call-start = ((), (), s32[]{:S(2)}) async-start(), calls=%async_computation.7 | async-start | bytes 1572864 | tf_op jit(solution)/shard_map/all_gather | solution.py:106
  162.1 36.3 %all-reduce.35.cloned.1.call-start = ((), (), s32[]{:S(2)}) async-start(), calls=%async_computation.8 | async-start | bytes 2097152 | tf_op jit(solution)/shard_map/psum | solution.py:91
  175.9 24.0 %copy-start.13 = (bf16[1024,512]{1,0:T(8,128)(2,1)S(1)}, bf16[1024,512]{1,0:T(8,128)(2,1)}, u32[]{:S(2)}) copy-start(bf16[1024,512]{1,0:T(8,128)(2,1)} %param.19) | copy-start | bytes 3145732
  177.7 38.6 %reduce-scatter.7.cloned.1.call-start = ((), (), s32[]{:S(2)}) async-start(), calls=%async_computation.9 | async-start | bytes 1572864 | tf_op jit(solution)/shard_map/reduce_scatter | solution.py:98
  206.5 21.4 %all-gather.8.cloned.1.call-start = ((), (), s32[]{:S(2)}) async-start(), calls=%async_computation.10 | async-start | bytes 1572864 | tf_op jit(solution)/shard_map/all_gather | solution.py:106
  216.3 36.3 %all-reduce.37.cloned.1.call-start = ((), (), s32[]{:S(2)}) async-start(), calls=%async_computation.11 | async-start | bytes 2097152 | tf_op jit(solution)/shard_map/psum | solution.py:91
  230.1 24.0 %copy-start.14 = (bf16[1024,512]{1,0:T(8,128)(2,1)S(1)}, bf16[1024,512]{1,0:T(8,128)(2,1)}, u32[]{:S(2)}) copy-start(bf16[1024,512]{1,0:T(8,128)(2,1)} %param.19) | copy-start | bytes 3145732
  231.8 38.7 %reduce-scatter.9.cloned.1.call-start = ((), (), s32[]{:S(2)}) async-start(), calls=%async_computation.12 | async-start | bytes 1572864 | tf_op jit(solution)/shard_map/reduce_scatter | solution.py:98
  257.1 25.2 %copy-start.8 = (bf16[1024,512]{1,0:T(8,128)(2,1)S(1)}, bf16[1024,512]{1,0:T(8,128)(2,1)}, u32[]{:S(2)}) copy-start(bf16[1024,512]{1,0:T(8,128)(2,1)} %param.15) | copy-start | bytes 3145732
  260.8 21.5 %all-gather.10.cloned.1.call-start = ((), (), s32[]{:S(2)}) async-start(), calls=%async_computation.13 | async-start | bytes 1572864 | tf_op jit(solution)/shard_map/all_gather | solution.py:106
  270.5 36.0 %all-reduce.39.cloned.1.call-start = ((), (), s32[]{:S(2)}) async-start(), calls=%async_computation.14 | async-start | bytes 2097152 | tf_op jit(solution)/shard_map/psum | solution.py:91
  285.7 22.3 %copy-start.15 = (bf16[1024,512]{1,0:T(8,128)(2,1)S(1)}, bf16[1024,512]{1,0:T(8,128)(2,1)}, u32[]{:S(2)}) copy-start(bf16[1024,512]{1,0:T(8,128)(2,1)} %param.19) | copy-start | bytes 3145732
  285.8 38.6 %reduce-scatter.11.cloned.1.call-start = ((), (), s32[]{:S(2)}) async-start(), calls=%async_computation.15 | async-start | bytes 1572864 | tf_op jit(solution)/shard_map/reduce_scatter | solution.py:98
  311.0 3.7 %copy-start.2 = (bf16[512,512]{1,0:T(8,128)(2,1)S(1)}, bf16[512,512]{1,0:T(8,128)(2,1)}, u32[]{:S(2)}) copy-start(bf16[512,512]{1,0:T(8,128)(2,1)} %reduce-scatter.5.cloned.1.call-done) | copy-start | bytes 1572868
  314.7 3.2 copy-start.3
  324.4 2.2 copy-start.1
Sparse Core Ops, SparseCore 0:
  125.7 18.4 all-reduce.32
  152.5 9.5 reduce-scatter.4
  163.6 10.1 all-gather.5
  177.8 20.5 all-reduce.34
  206.6 9.5 reduce-scatter.6
  217.6 10.1 all-gather.7
  232.0 20.5 all-reduce.36
  260.9 9.5 reduce-scatter.8
  272.1 10.1 all-gather.9
  285.9 20.5 all-reduce.38
  314.8 9.5 reduce-scatter.10
where the time goes:
time: 340 us; the launch traced here: 339 us
  waiting for transfers between devices  149 us (44%)
  blocking collectives  78.5 us (23%)
  matrix products  41.5 us (12%)
  local copies, waits for them, and re-layouts  31.1 us (9%)
  other arithmetic  24 us (7%)
  between operations  14.1 us (4%)
    psum x4, waiting for transfers between devices, per_device(): lax.psum(jnp.dot(current.astype(jnp.bfloat16), readout_w, preferred_eleme...  80.3 us
    all_gather x2, blocking collectives, carried_in(): pieces = jax.tree.map(lambda part: lax.all_gather(part, axis), value)  63 us
    all_gather x3, waiting for transfers between devices, per_device(): full_guess = lax.all_gather(guessed, 'mp', axis=1, tiled=True)  35 us
    reduce_scatter x4, waiting for transfers between devices, per_device(): lax.psum_scatter(jnp.dot(hidden, w_out, preferred_element_type=jnp.float3...  33.6 us
    all_to_all x1, blocking collectives, per_device(): lax.all_to_all(shortened(corrected.reshape(batch, 1, steps, width_part)),...  15.5 us
    dot_general x4, matrix products, per_device(): jnp.dot(hidden, w_out, preferred_element_type=jnp.float32)  14.6 us
    pad x24, local copies, waits for them, and re-layouts, per_device(): lax.associative_scan(combine, (gates, driven), axis=1)  12.2 us
    dot_general x4, matrix products, hidden_units(): jnp.dot(normed, w_hidden, preferred_element_type=jnp.float32)  11.8 us
  transfers between devices with their start and end apart: 11, of which 11 were waited for; matrix products, arithmetic and copies ran while one was open for 2% of the time, Pallas kernels for 0%

commit v1 on v0

--- a/solution.py
+++ b/solution.py
@@ -88,11 +88,14 @@
     action_rows = actions.reshape(rows, horizon)
     outputs = []
     for step in range(horizon):
-        features = lax.psum(
-            jnp.dot(
-                current.astype(jnp.bfloat16), readout_w, preferred_element_type=jnp.float32
-            ).astype(jnp.bfloat16),
-            "mp",
+        features = jnp.sum(
+            lax.all_gather(
+                jnp.dot(
+                    current.astype(jnp.bfloat16), readout_w, preferred_element_type=jnp.float32
+                ).astype(jnp.bfloat16),
+                axis_name="mp",
+            ),
+            axis=0,
         ).astype(jnp.float32)
         hidden = hidden_units(features, norm_gain, w_hidden, action_embed, action_rows[:, step])
         guessed = lax.psum_scatter(

time: 340 us -> 306 us (0.900)
  waiting for transfers between devices: 149 us -> 113 us
  other arithmetic: 24 us -> 27.9 us
    psum x4 -> x0, waiting for transfers between devices: 80.3 us -> none  [per_device(): lax.psum(jnp.dot(current.astype(jnp.bfloat16), readout_w, preferred_eleme...]
    all_gather x0 -> x4, waiting for transfers between devices: none -> 44.7 us  [per_device(): lax.all_gather(jnp.dot(current.astype(jnp.bfloat16), readout_w, preferred...]
    reduce_sum x0 -> x4, other arithmetic: none -> 8.81 us  [per_device(): jnp.sum(lax.all_gather(jnp.dot(current.astype(jnp.bfloat16), readout_w, p...]
    reduce_sum x4, other arithmetic: 6.01 us -> 1.12 us  [hidden_units(): mean_sq = jnp.mean(features * features, axis=-1, keepdims=True)]
where the time goes in v1:
time: 306 us; the launch traced here: 305 us
  waiting for transfers between devices  113 us (37%)
  blocking collectives  78.5 us (26%)
  matrix products  39 us (13%)
  local copies, waits for them, and re-layouts  31.1 us (10%)
  other arithmetic  27.9 us (9%)
  between operations  14.1 us (5%)
    all_gather x2, blocking collectives, carried_in(): pieces = jax.tree.map(lambda part: lax.all_gather(part, axis), value)  63 us
    all_gather x4, waiting for transfers between devices, per_device(): lax.all_gather(jnp.dot(current.astype(jnp.bfloat16), readout_w, preferred...  44.7 us
    all_gather x3, waiting for transfers between devices, per_device(): full_guess = lax.all_gather(guessed, 'mp', axis=1, tiled=True)  35 us
    reduce_scatter x4, waiting for transfers between devices, per_device(): lax.psum_scatter(jnp.dot(hidden, w_out, preferred_element_type=jnp.float3...  33.5 us
    all_to_all x1, blocking collectives, per_device(): lax.all_to_all(shortened(corrected.reshape(batch, 1, steps, width_part)),...  15.5 us
    dot_general x4, matrix products, per_device(): jnp.dot(hidden, w_out, preferred_element_type=jnp.float32)  14.6 us
    pad x24, local copies, waits for them, and re-layouts, per_device(): lax.associative_scan(combine, (gates, driven), axis=1)  12.2 us
    dot_general x4, matrix products, hidden_units(): jnp.dot(normed, w_hidden, preferred_element_type=jnp.float32)  9.39 us
  transfers between devices with their start and end apart: 11, of which 11 were waited for; matrix products, arithmetic and copies ran while one was open for 2% of the time, Pallas kernels for 0%

profile of v1, /device:TPU:0, one launch (start us, length us, event | category | flops | bytes accessed | tf_op | source)
XLA Modules:
  0.0 304.9 jit_solution(11662835133420371287)
XLA Ops:
  8.8 1.5 slice.219
  10.3 2.2 convolution_multiply_fusion.3
  12.6 1.5 slice.268
  14.1 1.5 slice.222
  15.6 1.4 slice.221
  17.0 1.4 multiply_add_fusion
  25.9 1.2 fusion.36
  29.0 2.0 pad.98
  31.0 4.3 %pad.99 = f32[4,128,512]{2,1,0:T(8,128)} pad(f32[4,64,512]{2,1,0:T(8,128)} %add.264, f32[]{:T(128)} %constant.56.clone.1), padding=0_0_0x1_0_1x0_0_0 | pad | bytes 1572868 | tf_op jit(solution)/shard_map/pad | solution.py:70
  36.2 32.4 %all-gather.1 = f32[32,1,512]{2,1,0:T(1,128)S(1)} all-gather(f32[4,1,512]{2,1,0:T(1,128)S(1)} %slice_add_fusion), channel_id=3, replica_groups=mesh['rep'=2,'tm'=8,'mp'=2] {'tm'}, dimensions={0}, use_global_device_ids=true | all-gather | bytes 73728 | tf_op jit(solution)/shard_map/all_gather | solution.py:9
  68.7 4.3 %pad.113 = f32[4,128,512]{2,1,0:T(8,128)} pad(f32[4,64,512]{2,1,0:T(8,128)} %add.272, f32[]{:T(128)} %constant.56.clone.1), padding=0_0_0x1_0_1x0_0_0 | pad | bytes 1572868 | tf_op jit(solution)/shard_map/pad | solution.py:70
  73.8 30.7 %all-gather = f32[32,1,512]{2,1,0:T(1,128)S(1)} all-gather(f32[4,1,512]{2,1,0:T(1,128)S(1)} %slice_add_fusion.1), channel_id=2, replica_groups=mesh['rep'=2,'tm'=8,'mp'=2] {'tm'}, dimensions={0}, use_global_device_ids=true | all-gather | bytes 73728 | tf_op jit(solution)/shard_map/all_gather | solution.py:9
  105.0 2.0 fusion.35
  107.5 15.5 %all_to_all.4 = bf16[4,1,128,512]{3,0,1,2:T(4,128)(2,1)S(1)} all-to-all(bf16[4,1,128,512]{3,0,1,2:T(4,128)(2,1)S(1)} %copy.27), channel_id=1, replica_groups=mesh['rep'=2,'tm'=8,'mp'=2] {'tm'}, dimensions={2} | all-to-all | bytes 1048576 | tf_op jit(solution)/shard_map/all_to_all | solution.py:78
  123.8 1.7 convolution_convert_fusion.7
  125.7 9.5 %all-gather.20.cloned.1.call-done = bf16[1024,1024]{1,0:T(8,128)(2,1)} async-done(((bf16[512,1024]{1,0:T(8,128)(2,1)}), bf16[1024,1024]{1,0:T(8,128)(2,1)}) %all-gather.20.cloned.1.call-update) | async-done | bytes 2097168 | tf_op jit(solution)/shard_map/all_gather | solution.py:92
  135.3 2.2 reduce_sum.84
  137.8 1.7 fusion.23
  139.6 3.7 %convolution_convert_fusion.6 = bf16[512,1024]{1,0:T(8,128)(2,1)} fusion(bf16[512,1024]{1,0:T(8,128)(2,1)} %param.21, f32[512,512]{1,0:T(8,128)} %fusion.23, bf16[18,512]{1,0:T(8,128)(2,1)S(1)} %copy-done.14, s32[512]{0:T(512)S(1)} %bitcast.99), kind=kOutput, calls=%fused_computation.30 | convolution fusion | flops 548414464 | bytes 3166208 | tf_op jit(solution)/shard_map/dot_general | solution.py:102
  143.3 9.7 %reduce-scatter.5.cloned.1.call-done = bf16[512,512]{1,0:T(8,128)(2,1)} async-done(((bf16[512,1024]{1,0:T(8,128)(2,1)}), bf16[512,512]{1,0:T(8,128)(2,1)}) %reduce-scatter.5.cloned.1.call-update) | async-done | bytes 524304 | tf_op jit(solution)/shard_map/reduce_scatter | solution.py:101
  153.1 11.7 %all-gather.14.cloned.1.call-done = bf16[512,1024]{1,0:T(8,128)(2,1)} async-done(((bf16[512,512]{1,0:T(8,128)(2,1)}), bf16[512,1024]{1,0:T(8,128)(2,1)}) %all-gather.14.cloned.1.call-update) | async-done | bytes 1048592 | tf_op jit(solution)/shard_map/all_gather | solution.py:109
  164.8 2.1 fusion.15
  166.8 1.7 convolution_convert_fusion.5
  168.8 11.7 %all-gather.22.cloned.1.call-done = bf16[1024,1024]{1,0:T(8,128)(2,1)} async-done(((bf16[512,1024]{1,0:T(8,128)(2,1)}), bf16[1024,1024]{1,0:T(8,128)(2,1)}) %all-gather.22.cloned.1.call-update) | async-done | bytes 2097168 | tf_op jit(solution)/shard_map/all_gather | solution.py:92
  180.5 2.2 reduce_sum.86
  182.9 3.0 fusion.21
  185.9 3.6 %convolution_convert_fusion.4 = bf16[512,1024]{1,0:T(8,128)(2,1)} fusion(bf16[512,1024]{1,0:T(8,128)(2,1)} %param.21, f32[512,512]{1,0:T(8,128)} %fusion.21, bf16[18,512]{1,0:T(8,128)(2,1)S(1)} %copy-done.14, s32[512]{0:T(512)S(1)} %bitcast.98), kind=kOutput, calls=%fused_computation.28 | convolution fusion | flops 548414464 | bytes 3166208 | tf_op jit(solution)/shard_map/dot_general | solution.py:102
  189.5 9.7 %reduce-scatter.7.cloned.1.call-done = bf16[512,512]{1,0:T(8,128)(2,1)} async-done(((bf16[512,1024]{1,0:T(8,128)(2,1)}), bf16[512,512]{1,0:T(8,128)(2,1)}) %reduce-scatter.7.cloned.1.call-update) | async-done | bytes 524304 | tf_op jit(solution)/shard_map/reduce_scatter | solution.py:101
  199.2 11.6 %all-gather.16.cloned.1.call-done = bf16[512,1024]{1,0:T(8,128)(2,1)} async-done(((bf16[512,512]{1,0:T(8,128)(2,1)}), bf16[512,1024]{1,0:T(8,128)(2,1)}) %all-gather.16.cloned.1.call-update) | async-done | bytes 1048592 | tf_op jit(solution)/shard_map/all_gather | solution.py:109
  210.8 2.2 fusion.14
  213.1 1.7 convolution_convert_fusion.3
  214.8 11.9 %all-gather.24.cloned.1.call-done = bf16[1024,1024]{1,0:T(8,128)(2,1)} async-done(((bf16[512,1024]{1,0:T(8,128)(2,1)}), bf16[1024,1024]{1,0:T(8,128)(2,1)}) %all-gather.24.cloned.1.call-update) | async-done | bytes 2097168 | tf_op jit(solution)/shard_map/all_gather | solution.py:92
  226.7 2.2 reduce_sum.88
  229.1 3.0 fusion.19
  232.1 3.7 %convolution_convert_fusion.2 = bf16[512,1024]{1,0:T(8,128)(2,1)} fusion(bf16[512,1024]{1,0:T(8,128)(2,1)} %param.21, f32[512,512]{1,0:T(8,128)} %fusion.19, bf16[18,512]{1,0:T(8,128)(2,1)S(1)} %copy-done.14, s32[512]{0:T(512)S(1)} %bitcast.97), kind=kOutput, calls=%fused_computation.26 | convolution fusion | flops 548414464 | bytes 3166208 | tf_op jit(solution)/shard_map/dot_general | solution.py:102
  235.8 9.7 %reduce-scatter.9.cloned.1.call-done = bf16[512,512]{1,0:T(8,128)(2,1)} async-done(((bf16[512,1024]{1,0:T(8,128)(2,1)}), bf16[512,512]{1,0:T(8,128)(2,1)}) %reduce-scatter.9.cloned.1.call-update) | async-done | bytes 524304 | tf_op jit(solution)/shard_map/reduce_scatter | solution.py:101
  245.6 11.7 %all-gather.18.cloned.1.call-done = bf16[512,1024]{1,0:T(8,128)(2,1)} async-done(((bf16[512,512]{1,0:T(8,128)(2,1)}), bf16[512,1024]{1,0:T(8,128)(2,1)}) %all-gather.18.cloned.1.call-update) | async-done | bytes 1048592 | tf_op jit(solution)/shard_map/all_gather | solution.py:109
  257.3 3.5 %convolution_convert_fusion.1 = bf16[512,1024]{1,0:T(8,128)(2,1)} fusion(bf16[512,1024]{1,0:T(8,128)(2,1)S(1)} %copy-done, bf16[512,1024]{1,0:T(8,128)(2,1)} %all-gather.18.cloned.1.call-done, bf16[1024,512]{1,0:T(8,128)(2,1)S(1)} %copy-done.8, f32[512,512]{1,0:T(8,128)S(1)} %fusion.14, f32[512]{0:T(512)S(1)} %get-tuple-element.128, ...), kind=kOutput, calls=%fused_computation.25 | convolution fusion | flops 1075314688 | bytes 5246976 | tf_op jit(solution)/shard_map/dot_general | solution.py:93
  261.0 11.6 %all-gather.26.cloned.1.call-done = bf16[1024,1024]{1,0:T(8,128)(2,1)} async-done(((bf16[512,1024]{1,0:T(8,128)(2,1)}), bf16[1024,1024]{1,0:T(8,128)(2,1)}) %all-gather.26.cloned.1.call-update) | async-done | bytes 2097168 | tf_op jit(solution)/shard_map/all_gather | solution.py:92
  272.7 2.2 reduce_sum.90
  275.2 1.7 fusion.17
  277.0 3.6 %convolution_convert_fusion = bf16[512,1024]{1,0:T(8,128)(2,1)} fusion(bf16[512,1024]{1,0:T(8,128)(2,1)} %param.21, f32[512,512]{1,0:T(8,128)} %fusion.17, bf16[18,512]{1,0:T(8,128)(2,1)S(1)} %copy-done.14, s32[512]{0:T(512)S(1)} %bitcast.96), kind=kOutput, calls=%fused_computation.24 | convolution fusion | flops 548414464 | bytes 3166208 | tf_op jit(solution)/shard_map/dot_general | solution.py:102
  280.7 1.0 copy.30
  281.7 2.1 copy.31
  283.8 2.0 copy.32
  285.8 4.5 %reduce-scatter.11.cloned.1.call-done = bf16[512,512]{1,0:T(8,128)(2,1)} async-done(((bf16[512,1024]{1,0:T(8,128)(2,1)}), bf16[512,512]{1,0:T(8,128)(2,1)}) %reduce-scatter.11.cloned.1.call-update) | async-done | bytes 524304 | tf_op jit(solution)/shard_map/reduce_scatter | solution.py:101
  290.3 2.2 copy.33
  292.5 5.9 %pad_maximum_fusion = bf16[4,8,16,4,512]{4,3,2,1,0:T(4,128)(2,1)} fusion(bf16[4,8,16,1,512]{4,3,2,1,0:T(2,128)(2,1)S(1)} %copy.33, bf16[4,8,16,1,512]{4,3,2,1,0:T(2,128)(2,1)S(1)} %copy-done.1, bf16[4,8,16,1,512]{4,3,2,1,0:T(2,128)(2,1)S(1)} %copy.31, bf16[4,8,16,1,512]{4,3,2,1,0:T(2,128)(2,1)S(1)} %copy.30), kind=kLoop, calls=%fused_computation.23 | loop fusion | flops 8388608 | bytes 4194304 | tf_op jit(solution)/shard_map/stack | solution.py:113
  (179 shorter events, 17.1 us)
Async XLA Ops:
  6.5 117.3 %copy-start = (bf16[512,1024]{1,0:T(8,128)(2,1)S(1)}, bf16[512,1024]{1,0:T(8,128)(2,1)}, u32[]{:S(2)}) copy-start(bf16[512,1024]{1,0:T(8,128)(2,1)} %param.17) | copy-start | bytes 3145732
  6.5 128.7 %all-gather.20.cloned.1.call-start = ((), (), s32[]{:S(2)}) async-start(), calls=%async_computation.12 | async-start | bytes 3145728 | tf_op jit(solution)/shard_map/all_gather | solution.py:92
  22.4 1.0 copy-start.9
  24.1 1.8 copy-start.4
  24.1 1.8 copy-start.5
  27.0 1.0 copy-start.6
  123.0 0.8 copy-start.10
  123.0 2.5 copy-start.11
  125.5 27.4 %reduce-scatter.5.cloned.1.call-start = ((), (), s32[]{:S(2)}) async-start(), calls=%async_computation.5 | async-start | bytes 1572864 | tf_op jit(solution)/shard_map/reduce_scatter | solution.py:101
  135.3 2.6 copy-start.12
  135.3 2.6 copy-start.15
  137.8 1.8 copy-start.14
  139.6 25.2 %copy-start.7 = (bf16[1024,512]{1,0:T(8,128)(2,1)S(1)}, bf16[1024,512]{1,0:T(8,128)(2,1)}, u32[]{:S(2)}) copy-start(bf16[1024,512]{1,0:T(8,128)(2,1)} %param.15) | copy-start | bytes 3145732
  143.3 21.5 %all-gather.14.cloned.1.call-start = ((), (), s32[]{:S(2)}) async-start(), calls=%async_computation.6 | async-start | bytes 1572864 | tf_op jit(solution)/shard_map/all_gather | solution.py:109
  153.0 27.5 %all-gather.22.cloned.1.call-start = ((), (), s32[]{:S(2)}) async-start(), calls=%async_computation.13 | async-start | bytes 3145728 | tf_op jit(solution)/shard_map/all_gather | solution.py:92
  168.6 30.6 %reduce-scatter.7.cloned.1.call-start = ((), (), s32[]{:S(2)}) async-start(), calls=%async_computation.7 | async-start | bytes 1572864 | tf_op jit(solution)/shard_map/reduce_scatter | solution.py:101
  189.5 21.3 %all-gather.16.cloned.1.call-start = ((), (), s32[]{:S(2)}) async-start(), calls=%async_computation.8 | async-start | bytes 1572864 | tf_op jit(solution)/shard_map/all_gather | solution.py:109
  199.2 27.5 %all-gather.24.cloned.1.call-start = ((), (), s32[]{:S(2)}) async-start(), calls=%async_computation.14 | async-start | bytes 3145728 | tf_op jit(solution)/shard_map/all_gather | solution.py:92
  214.8 30.7 %reduce-scatter.9.cloned.1.call-start = ((), (), s32[]{:S(2)}) async-start(), calls=%async_computation.9 | async-start | bytes 1572864 | tf_op jit(solution)/shard_map/reduce_scatter | solution.py:101
  232.1 25.2 %copy-start.8 = (bf16[1024,512]{1,0:T(8,128)(2,1)S(1)}, bf16[1024,512]{1,0:T(8,128)(2,1)}, u32[]{:S(2)}) copy-start(bf16[1024,512]{1,0:T(8,128)(2,1)} %param.15) | copy-start | bytes 3145732
  235.8 21.5 %all-gather.18.cloned.1.call-start = ((), (), s32[]{:S(2)}) async-start(), calls=%async_computation.10 | async-start | bytes 1572864 | tf_op jit(solution)/shard_map/all_gather | solution.py:109
  245.5 27.2 %all-gather.26.cloned.1.call-start = ((), (), s32[]{:S(2)}) async-start(), calls=%async_computation.15 | async-start | bytes 3145728 | tf_op jit(solution)/shard_map/all_gather | solution.py:92
  260.8 29.6 %reduce-scatter.11.cloned.1.call-start = ((), (), s32[]{:S(2)}) async-start(), calls=%async_computation.11 | async-start | bytes 1572864 | tf_op jit(solution)/shard_map/reduce_scatter | solution.py:101
  272.7 2.5 copy-start.13
  277.0 3.7 %copy-start.2 = (bf16[512,512]{1,0:T(8,128)(2,1)S(1)}, bf16[512,512]{1,0:T(8,128)(2,1)}, u32[]{:S(2)}) copy-start(bf16[512,512]{1,0:T(8,128)(2,1)} %reduce-scatter.5.cloned.1.call-done) | copy-start | bytes 1572868
  280.6 3.2 %copy-start.3 = (bf16[512,512]{1,0:T(8,128)(2,1)S(1)}, bf16[512,512]{1,0:T(8,128)(2,1)}, u32[]{:S(2)}) copy-start(bf16[512,512]{1,0:T(8,128)(2,1)} %reduce-scatter.9.cloned.1.call-done) | copy-start | bytes 1572868
  290.3 2.2 copy-start.1
Sparse Core Ops, SparseCore 0:
  125.7 9.5 all-gather.19
  143.4 9.5 reduce-scatter.4
  154.5 10.1 all-gather.13
  168.7 11.7 all-gather.21
  189.6 9.5 reduce-scatter.6
  200.6 10.1 all-gather.15
  214.9 11.7 all-gather.23
  235.9 9.5 reduce-scatter.8
  247.0 10.1 all-gather.17
  260.9 11.7 all-gather.25
  280.8 9.5 reduce-scatter.10
